TPU v7x, 32 devices: a whole 2x2x4 slice. The times are simulated.
32 devices in a mesh: groups: 2 (over y), dp: 4 (over z), tensor: 2 (over x), layer: 2 (over core).
Axes of the slice: x: 2, y: 2, z: 4, core: 2. Of those that a mesh axis runs over, the one named last changes fastest.
Arguments:
- hidden_in: bfloat16 [2, 8, 512, 14336], P('layer', ('groups', 'dp'), None, 'tensor'), parts along dimension 1, may hold values from -6 to 6
- out_grad: bfloat16 [2, 8, 512, 4096], P('layer', ('groups', 'dp'), 'tensor'), parts along dimension 1, may hold values from -6 to 6
- proj_in: bfloat16 [2, 14336, 64], P('layer', 'tensor'), may hold values from -0.046875 to 0.046875
- proj_out: bfloat16 [2, 4096, 64], P('layer'), may hold values from -0.09375 to 0.09375
- query_grads: bfloat16 [2, 1024, 4096], P('layer', 'dp', 'tensor'), may hold values from -1.5 to 1.5
- lengths: int32 [8], P(('groups', 'dp')), parts along dimension 0, may hold values from 128 to 512, as said below
- query_decision: int32 [1024], P('dp'), may hold values from 0 to 1023
Outputs:
- influence: float32 [8, 1024], P(('groups', 'dp')), parts along dimension 0
There are 2 independent parts, one for each index of `groups`. A program takes and returns all parts, laid end to end along the dimension named above; an argument that names none is the same for every part. Nothing has to cross between parts.
Inputs may be any that keep to these rules, and one draw needn't show every extreme that they name: `lengths`: in each part one transcript has all 512 tokens live and another has exactly 128.
All inputs are finite; a program needn't handle non-finite values.
Results may differ from a plain program's by a relative error of at most 0.004.
Values may be sent and summed in bfloat16 or wider, within the bound.
No kernel may reach another device: no remote copies, remote signals or barrier semaphores. Data moves between devices by JAX's collectives and lax.ppermute only.
A program may use at most 64 MiB of HBM per device.

v0:
```python
import jax
import jax.numpy as jnp
from jax import lax
from jax.sharding import PartitionSpec as P

DECISIONS = 1024


def decision_table(decisions):
    return (decisions[:, None] == jnp.arange(DECISIONS, dtype=jnp.int32)[None, :]).astype(
        jnp.float32
    )


def body(hidden_in, out_grad, proj_in, proj_out, query_grads, lengths, query_decision):
    hidden_rows = hidden_in[0]
    grad_rows = out_grad[0]
    side_hidden = proj_in[0]
    side_width = proj_out[0]
    query_rows = query_grads[0]
    ex_count = hidden_rows.shape[0]
    seq_shard = grad_rows.shape[1]
    first_pos = lax.axis_index("tensor") * seq_shard
    positions = first_pos + jnp.arange(seq_shard, dtype=jnp.int32)
    live_tokens = (positions[None, :] < lengths[:, None]).astype(jnp.float32)
    right = jnp.einsum("etd,dp->etp", grad_rows, side_width, preferred_element_type=jnp.float32)
    right = (right * live_tokens[:, :, None]).astype(jnp.bfloat16)
    left = jnp.einsum("etf,fp->etp", hidden_rows, side_hidden, preferred_element_type=jnp.float32)
    left_own = lax.psum_scatter(left, "tensor", scatter_dimension=1, tiled=True)
    partial_value = jnp.einsum(
        "etp,etq->epq", left_own, right.astype(jnp.float32), precision=lax.Precision.HIGHEST
    )
    partial_value = partial_value / lengths.astype(jnp.float32)[:, None, None]
    grad_part = lax.psum_scatter(partial_value, "tensor", scatter_dimension=1, tiled=True)
    grad_flat = grad_part.reshape(ex_count, -1).astype(jnp.bfloat16)
    block_rows = lax.all_gather(query_rows, "dp", axis=0, tiled=True)
    block_decisions = lax.all_gather(query_decision, "dp", axis=0, tiled=True)
    scores = jnp.einsum("ek,qk->eq", grad_flat, block_rows, preferred_element_type=jnp.float32)
    partial_dec = jnp.dot(scores, decision_table(block_decisions), precision=lax.Precision.HIGHEST)
    result = lax.psum(partial_dec, ("tensor", "layer"))
    return result


def solution(mesh):
    in_specs = (
        P("layer", ("groups", "dp"), None, "tensor"),
        P("layer", ("groups", "dp"), "tensor", None),
        P("layer", "tensor", None),
        P("layer", None, None),
        P("layer", "dp", "tensor"),
        P(("groups", "dp")),
        P("dp"),
    )
    out_specs = P(("groups", "dp"), None)
    return jax.shard_map(body, mesh=mesh, in_specs=in_specs, out_specs=out_specs, check_vma=False)
```

profile of v0, /device:TPU:0, one launch (start us, length us, event | category | flops | bytes accessed | tf_op | source)
XLA Modules:
  0.0 130.6 jit_solution(11717772726066423702)
XLA Ops:
  7.4 0.0 copy-start
  7.4 0.0 copy-start.2
  7.4 0.0 copy-start.1
  7.4 0.0 reduce-scatter.3.cloned.1.call-start
  7.4 6.4 %fusion.11 = f32[1,512,64]{1,2,0:T(8,128)} fusion(bf16[1,1,512,7168]{3,2,1,0:T(8,128)(2,1)} %param.7, bf16[1,7168,64]{1,2,0:T(8,128)(2,1)} %param.9), kind=kOutput, calls=%fused_computation.10 | convolution fusion | flops 469762048 | bytes 8388608 | tf_op jit(solution)/shard_map/etf,fp->etp/dot_general | solution.py:28
  13.8 0.0 reduce-scatter.3.cloned.1.call-update
  13.8 0.0 reduce-scatter.5.cloned.1.call-start
  14.5 0.0 copy-done
  14.5 0.0 copy-done.2
  14.6 0.7 fusion.14
  15.2 11.8 %reduce-scatter.3.cloned.1.call-done = f32[1,256,64]{1,2,0:T(8,128)} async-done(((f32[1,512,64]{1,2,0:T(8,128)}), f32[1,256,64]{1,2,0:T(8,128)}) %reduce-scatter.3.cloned.1.call-update) | async-done | bytes 65552 | tf_op jit(solution)/shard_map/reduce_scatter | solution.py:29
  27.1 1.6 %fusion.17 = f32[1,64,64]{2,1,0:T(8,128)} fusion(bf16[256,64]{1,0:T(8,128)(2,1)S(1)} %fusion.14, f32[1,256,64]{1,2,0:T(8,128)} %reduce-scatter.3.cloned.1.call-done, f32[]{:T(128)} %bitcast.7), kind=kOutput, calls=%fused_computation.13 | convolution fusion | flops 12587008 | bytes 114692 | tf_op jit(solution)/shard_map/etp,etq->epq/dot_general | solution.py:30
  28.7 0.0 reduce-scatter.5.cloned.1.call-update
  28.7 0.0 all-gather.4.cloned.1.call-start
  28.7 0.5 all-gather.4.cloned.1.call-update
  29.3 0.0 copy-done.1
  29.3 10.9 %all-gather.1 = s32[4,1,256]{2,1,0:T(1,128)S(1)} all-gather(s32[1,1,256]{2,1,0:T(1,128)S(1)} %bitcast.43), channel_id=1, replica_groups=mesh['groups'=2,'dp'=4,'tensor'=2,'layer'=2] {'dp'}, dimensions={0}, use_global_device_ids=true | all-gather | bytes 5120 | tf_op jit(solution)/shard_map/all_gather | solution.py:37
  40.2 0.0 reduce-scatter.5.cloned.1.call-done
  40.2 0.7 convert_element_type.30
  40.9 0.1 reshape.54
  41.0 70.4 %all-gather.4.cloned.1.call-done = bf16[1,1024,2048]{2,1,0:T(8,128)(2,1)} async-done(((bf16[1,256,2048]{2,1,0:T(8,128)(2,1)}), bf16[1,1024,2048]{2,1,0:T(8,128)(2,1)}) %all-gather.4.cloned.1.call-update) | async-done | bytes 4194320 | tf_op jit(solution)/shard_map/all_gather | solution.py:36
  111.4 3.4 %fusion.18 = f32[1024,1]{0,1:T(1,128)S(1)} fusion(bf16[2048,1]{0,1:T(2,128)(2,1)S(1)} %reshape.54, bf16[1,1024,2048]{2,1,0:T(8,128)(2,1)} %all-gather.4.cloned.1.call-done), kind=kOutput, calls=%fused_computation.14 | convolution fusion | flops 4194304 | bytes 4202496 | tf_op jit(solution)/shard_map/ek,qk->eq/dot_general | solution.py:38
  114.7 1.5 %fusion.4 = f32[1,1024]{1,0:T(1,128)S(1)} fusion(f32[1024,1]{0,1:T(1,128)S(1)} %fusion.18, s32[1024]{0:T(1024)S(1)} %bitcast.42), kind=kOutput, calls=%fused_computation.5 | convolution fusion | flops 13631488 | bytes 12288 | tf_op jit(solution)/shard_map/dot_general | solution.py:39
  116.2 7.0 %psum.7 = f32[1,1024]{1,0:T(1,128)} all-reduce(f32[1,1024]{1,0:T(1,128)S(1)} %fusion.4), channel_id=1, replica_groups=mesh['groups'=2,'dp'=4,'tensor'=2,'layer'=2] {'tensor','layer'}, use_global_device_ids=true, to_apply=%region_2.0 | all-reduce | flops 1024 | bytes 8192 | tf_op jit(solution)/shard_map/psum | solution.py:40
  (1 shorter events, 0.0 us)
Async XLA Ops:
  7.4 7.2 %copy-start = (bf16[1,1,256,4096]{3,2,1,0:T(8,128)(2,1)S(1)}, bf16[1,1,256,4096]{3,2,1,0:T(8,128)(2,1)}, u32[]{:S(2)}) copy-start(bf16[1,1,256,4096]{3,2,1,0:T(8,128)(2,1)} %param.8) | copy-start | bytes 6291460
  7.4 7.2 %copy-start.2 = (bf16[1,4096,64]{1,2,0:T(8,128)(2,1)S(1)}, bf16[1,4096,64]{1,2,0:T(8,128)(2,1)}, u32[]{:S(2)}) copy-start(bf16[1,4096,64]{1,2,0:T(8,128)(2,1)} %param.10) | copy-start | bytes 1572868
  7.4 21.9 %copy-start.1 = (s32[256]{0:T(256)S(1)}, s32[256]{0:T(256)}, u32[]{:S(2)}) copy-start(s32[256]{0:T(256)} %param.13) | copy-start | bytes 3076
  7.4 19.7 %reduce-scatter.3.cloned.1.call-start = ((), (), s32[]{:S(2)}) async-start(), calls=%async_computation.2 | async-start | bytes 196608 | tf_op jit(solution)/shard_map/reduce_scatter | solution.py:29
  13.8 26.4 %reduce-scatter.5.cloned.1.call-start = ((), (), s32[]{:S(2)}) async-start(), calls=%async_computation.3 | async-start | bytes 49152 | tf_op jit(solution)/shard_map/reduce_scatter | solution.py:34
  28.7 82.7 %all-gather.4.cloned.1.call-start = ((), (), s32[]{:S(2)}) async-start(), calls=%async_computation.4 | async-start | bytes 5242880 | tf_op jit(solution)/shard_map/all_gather | solution.py:36
Sparse Core Ops, SparseCore 0:
  13.9 13.0 reduce-scatter.2
  29.2 9.9 reduce-scatter.4
Sparse Core Ops, SparseCore 1:
  30.7 80.6 all-gather.3
where the time goes:
time: 131 us
  waiting for transfers between devices  82.7 us (63%)
  blocking collectives  17.9 us (14%)
  between operations  15.5 us (12%)
  matrix products  13.5 us (10%)
    all_gather x1, waiting for transfers between devices, body(): block_rows = lax.all_gather(query_rows, 'dp', axis=0, tiled=True)  70.4 us
    reduce_scatter x1, waiting for transfers between devices, body(): left_own = lax.psum_scatter(left, 'tensor', scatter_dimension=1, tiled=True)  11.8 us
    all_gather x1, blocking collectives, body(): block_decisions = lax.all_gather(query_decision, 'dp', axis=0, tiled=True)  10.9 us
    psum x1, blocking collectives, body(): result = lax.psum(partial_dec, ('tensor', 'layer'))  6.99 us
    dot_general x1, matrix products, body(): jnp.einsum('etf,fp->etp', hidden_rows, side_hidden, preferred_element_typ...  6.41 us
    dot_general x1, matrix products, body(): jnp.einsum('ek,qk->eq', grad_flat, block_rows, preferred_element_type=jnp...  3.37 us
  transfers between devices with their start and end apart: 3, of which 2 were waited for; matrix products, arithmetic and copies ran while one was open for 1% of the time, Pallas kernels for 0%

commit v1 on v0

--- a/solution.py
+++ b/solution.py
@@ -2,8 +2,31 @@
 import jax.numpy as jnp
 from jax import lax
 from jax.sharding import PartitionSpec as P
+from jax.lax import axis_index, axis_size, ppermute
 
 DECISIONS = 1024
+
+
+def handle_the_entries(payload, pos_dim):
+    arr_now = list(payload.shape[1:])
+    arr_now[pos_dim] *= payload.shape[0]
+    return jnp.moveaxis(payload, 0, pos_dim).reshape(arr_now)
+
+
+def test_the_chunk(array_dim, inner_x, dev_axis):
+    n_parts = axis_size(dev_axis)
+    leaves = [(src_i, (src_i + 1) % n_parts) for src_i in range(n_parts)]
+    left_arr, shaped = ([], [])
+    buffer = [(h, k) for k, h in leaves]
+    for p in range(n_parts - 1):
+        if p % 2 == 0:
+            left_arr.append(ppermute(left_arr[-1] if left_arr else inner_x, dev_axis, perm=leaves))
+        else:
+            shaped.append(ppermute(shaped[-1] if shaped else inner_x, dev_axis, buffer))
+    n_now = jnp.stack([*left_arr[::-1], inner_x, *shaped])
+    y1 = axis_index(dev_axis) - len(left_arr)
+    n_now = n_now[(jnp.arange(n_parts) - y1) % n_parts]
+    return handle_the_entries(n_now, array_dim)
 
 
 def decision_table(decisions):
@@ -33,7 +56,7 @@
     partial_value = partial_value / lengths.astype(jnp.float32)[:, None, None]
     grad_part = lax.psum_scatter(partial_value, "tensor", scatter_dimension=1, tiled=True)
     grad_flat = grad_part.reshape(ex_count, -1).astype(jnp.bfloat16)
-    block_rows = lax.all_gather(query_rows, "dp", axis=0, tiled=True)
+    block_rows = test_the_chunk(0, query_rows, "dp")
     block_decisions = lax.all_gather(query_decision, "dp", axis=0, tiled=True)
     scores = jnp.einsum("ek,qk->eq", grad_flat, block_rows, preferred_element_type=jnp.float32)
     partial_dec = jnp.dot(scores, decision_table(block_decisions), precision=lax.Precision.HIGHEST)

time: 131 us -> 114 us (0.87)
  waiting for transfers between devices: 82.7 us -> 53.2 us
  starting transfers between devices: 0.09 us -> 5.24 us
  local copies, waits for them, and re-layouts: 0.1 us -> 5.07 us
  other arithmetic: 0.73 us -> 4.32 us
  between operations: 15.5 us -> 14.1 us
    all_gather x1 -> x0, waiting for transfers between devices: 70.4 us -> none  [body(): block_rows = lax.all_gather(query_rows, 'dp', axis=0, tiled=True)]
    ppermute x0 -> x3, waiting for transfers between devices: none -> 24.3 us  [the longest x2 24.3 us: test_the_chunk(): ppermute(left_arr[-1] if left_arr else inner_x, dev_axis, perm=leaves)]
    reduce_scatter x1, waiting for transfers between devices: 11.8 us -> 28.8 us  [body(): left_own = lax.psum_scatter(left, 'tensor', scatter_dimension=1, tiled=True)]
    ppermute x0 -> x3, starting transfers between devices: none -> 5.2 us  [the longest x2 3.11 us: test_the_chunk(): ppermute(left_arr[-1] if left_arr else inner_x, dev_axis, perm=leaves)]
    gather x0 -> x1, local copies, waits for them, and re-layouts: none -> 4.97 us  [test_the_chunk(): n_now = n_now[(jnp.arange(n_parts) - y1) % n_parts]]
    another operation x0 -> x1, other arithmetic: none -> 3.58 us  [test_the_chunk(): n_now = jnp.stack([*left_arr[::-1], inner_x, *shaped])]
  transfers between devices with their start and end apart: 3 -> 5, of which waited for: 2 -> 2; matrix products, arithmetic and copies ran while one was open for 1% -> 9% of each run, Pallas kernels for 0% -> 0%
where the time goes in v1:
time: 114 us
  waiting for transfers between devices  53.2 us (47%)
  blocking collectives  17.4 us (15%)
  matrix products  14.4 us (13%)
  between operations  14.1 us (12%)
  starting transfers between devices  5.24 us (5%)
  local copies, waits for them, and re-layouts  5.07 us (4%)
  other arithmetic  4.32 us (4%)
    reduce_scatter x1, waiting for transfers between devices, body(): left_own = lax.psum_scatter(left, 'tensor', scatter_dimension=1, tiled=True)  28.8 us
    ppermute x2, waiting for transfers between devices, test_the_chunk(): ppermute(left_arr[-1] if left_arr else inner_x, dev_axis, perm=leaves)  24.3 us
    all_gather x1, blocking collectives, body(): block_decisions = lax.all_gather(query_decision, 'dp', axis=0, tiled=True)  10.9 us
    psum x1, blocking collectives, body(): result = lax.psum(partial_dec, ('tensor', 'layer'))  6.54 us
    dot_general x1, matrix products, body(): jnp.einsum('etf,fp->etp', hidden_rows, side_hidden, preferred_element_typ...  6.26 us
    gather x1, local copies, waits for them, and re-layouts, test_the_chunk(): n_now = n_now[(jnp.arange(n_parts) - y1) % n_parts]  4.97 us
    another operation x1, other arithmetic, test_the_chunk(): n_now = jnp.stack([*left_arr[::-1], inner_x, *shaped])  3.58 us
    dot_general x1, matrix products, body(): jnp.einsum('ek,qk->eq', grad_flat, block_rows, preferred_element_type=jnp...  3.37 us
  transfers between devices with their start and end apart: 5, of which 2 were waited for; matrix products, arithmetic and copies ran while one was open for 9% of the time, Pallas kernels for 0%

profile of v1, /device:TPU:0, one launch (start us, length us, event | category | flops | bytes accessed | tf_op | source)
XLA Modules:
  0.0 113.8 jit_solution(1224331434655017405)
XLA Ops:
  6.5 0.0 copy-start
  6.5 0.0 reduce-scatter.3.cloned.1.call-start
  6.5 3.1 %collective-permute-start = (bf16[256,2048]{1,0:T(8,128)(2,1)}, bf16[256,2048]{1,0:T(8,128)(2,1)}, u32[]{:S(2)}, u32[]{:S(2)}) collective-permute-start(bf16[256,2048]{1,0:T(8,128)(2,1)} %bitcast.46), channel_id=1, source_target_pairs={{0,4},{4,8},{8,12},{12,0},{1,5},{5,9},{9,13},{13,1},{2,6},{6,10},{... | collective-permute-start | bytes 3145736 | tf_op jit(solution)/shard_map/ppermute | solution.py:23
  9.7 2.1 %collective-permute-start.2 = (bf16[256,2048]{1,0:T(8,128)(2,1)}, bf16[256,2048]{1,0:T(8,128)(2,1)}, u32[]{:S(2)}, u32[]{:S(2)}) collective-permute-start(bf16[256,2048]{1,0:T(8,128)(2,1)} %bitcast.47), channel_id=1, source_target_pairs={{4,0},{8,4},{12,8},{0,12},{5,1},{9,5},{13,9},{1,13},{6,2},{10,6},{... | collective-permute-start | bytes 3145736 | tf_op jit(solution)/shard_map/ppermute | solution.py:25
  11.7 24.3 %collective-permute-done = bf16[256,2048]{1,0:T(8,128)(2,1)} collective-permute-done((bf16[256,2048]{1,0:T(8,128)(2,1)}, bf16[256,2048]{1,0:T(8,128)(2,1)}, u32[]{:S(2)}, u32[]{:S(2)}) %collective-permute-start) | collective-permute-done | bytes 1048608 | tf_op jit(solution)/shard_map/ppermute | solution.py:23
  36.1 0.0 collective-permute-start.1
  36.1 6.3 %fusion.9 = f32[1,512,64]{1,2,0:T(8,128)} fusion(bf16[1,1,512,7168]{3,2,1,0:T(8,128)(2,1)} %param.7, bf16[1,7168,64]{1,2,0:T(8,128)(2,1)} %param.9), kind=kOutput, calls=%fused_computation.10 | convolution fusion | flops 469762048 | bytes 8388608 | tf_op jit(solution)/shard_map/etf,fp->etp/dot_general | solution.py:51
  42.3 0.0 reduce-scatter.3.cloned.1.call-update
  42.3 0.0 reduce-scatter.5.cloned.1.call-start
  43.1 0.0 copy-done
  43.1 1.7 %fusion.12 = bf16[256,64]{1,0:T(8,128)(2,1)S(1)} fusion(bf16[1,1,256,4096]{3,2,1,0:T(8,128)(2,1)S(1)} %copy-done, bf16[1,4096,64]{1,2,0:T(8,128)(2,1)} %param.10, f32[256]{0:T(256)S(1)} %compare_convert_fusion), kind=kOutput, calls=%fused_computation.11 | convolution fusion | flops 134250496 | bytes 2655232 | tf_op jit(solution)/shard_map/etd,dp->etp/dot_general | solution.py:49
  44.8 28.8 %reduce-scatter.3.cloned.1.call-done = f32[1,256,64]{1,2,0:T(8,128)} async-done(((f32[1,512,64]{1,2,0:T(8,128)}), f32[1,256,64]{1,2,0:T(8,128)}) %reduce-scatter.3.cloned.1.call-update) | async-done | bytes 65552 | tf_op jit(solution)/shard_map/reduce_scatter | solution.py:52
  73.7 1.6 %fusion.15 = f32[1,64,64]{2,1,0:T(8,128)} fusion(bf16[256,64]{1,0:T(8,128)(2,1)S(1)} %fusion.12, f32[1,256,64]{1,2,0:T(8,128)} %reduce-scatter.3.cloned.1.call-done, f32[]{:T(128)} %bitcast.7), kind=kOutput, calls=%fused_computation.13 | convolution fusion | flops 12587008 | bytes 114692 | tf_op jit(solution)/shard_map/etp,etq->epq/dot_general | solution.py:53
  75.3 0.0 reduce-scatter.5.cloned.1.call-update
  75.3 10.9 %all-gather = s32[4,1,256]{2,1,0:T(1,128)S(1)} all-gather(s32[1,1,256]{2,1,0:T(1,128)S(1)} %bitcast.49), channel_id=1, replica_groups=mesh['groups'=2,'dp'=4,'tensor'=2,'layer'=2] {'dp'}, dimensions={0}, use_global_device_ids=true | all-gather | bytes 5120 | tf_op jit(solution)/shard_map/all_gather | solution.py:60
  86.2 0.7 convert_element_type.30
  86.9 0.1 reshape.114
  87.0 0.0 collective-permute-done.2
  87.0 0.0 collective-permute-done.1
  87.0 3.6 %pad_maximum_fusion = bf16[4,256,2048]{2,1,0:T(8,128)(2,1)} fusion(bf16[1,256,2048]{2,1,0:T(8,128)(2,1)} %bitcast.12, bf16[1,256,2048]{2,1,0:T(8,128)(2,1)S(1)} %copy-done.1, bf16[1,256,2048]{2,1,0:T(8,128)(2,1)} %bitcast.11, bf16[1,256,2048]{2,1,0:T(8,128)(2,1)} %bitcast.10), kind=kLoop, calls=%fused_computation.3 | loop fusion | flops 6291456 | bytes 8388608 | tf_op jit(solution)/shard_map/stack | solution.py:26
  90.6 5.0 %gather_fusion = bf16[4,256,2048]{2,1,0:T(8,128)(2,1)} fusion(bf16[4,256,2048]{2,1,0:T(8,128)(2,1)} %pad_maximum_fusion, s32[1024]{0:T(1024)S(1)} %pad_clamp_fusion), kind=kCustom, calls=%fused_computation | custom fusion | bytes 8388624 | tf_op jit(solution)/shard_map/gather | solution.py:28
  95.6 3.4 %convolution_bitcast_fusion = f32[1024,1]{0,1:T(1,128)S(1)} fusion(bf16[2048,1]{0,1:T(2,128)(2,1)S(1)} %reshape.114, bf16[1024,2048]{1,0:T(8,128)(2,1)} %bitcast.45), kind=kOutput, calls=%fused_computation.14 | convolution fusion | flops 4194304 | bytes 4202496 | tf_op jit(solution)/shard_map/ek,qk->eq/dot_general | solution.py:61
  99.0 1.5 %fusion.2 = f32[1,1024]{1,0:T(1,128)S(1)} fusion(f32[1024,1]{0,1:T(1,128)S(1)} %convolution_bitcast_fusion, s32[1024]{0:T(1024)S(1)} %bitcast.48), kind=kOutput, calls=%fused_computation.5 | convolution fusion | flops 13631488 | bytes 12288 | tf_op jit(solution)/shard_map/dot_general | solution.py:62
  100.4 6.5 %psum.7 = f32[1,1024]{1,0:T(1,128)} all-reduce(f32[1,1024]{1,0:T(1,128)S(1)} %fusion.2), channel_id=1, replica_groups=mesh['groups'=2,'dp'=4,'tensor'=2,'layer'=2] {'tensor','layer'}, use_global_device_ids=true, to_apply=%region_2.3 | all-reduce | flops 1024 | bytes 8192 | tf_op jit(solution)/shard_map/psum | solution.py:63
  (8 shorter events, 0.0 us)
Async XLA Ops:
  6.5 36.5 %copy-start = (bf16[1,1,256,4096]{3,2,1,0:T(8,128)(2,1)S(1)}, bf16[1,1,256,4096]{3,2,1,0:T(8,128)(2,1)}, u32[]{:S(2)}) copy-start(bf16[1,1,256,4096]{3,2,1,0:T(8,128)(2,1)} %param.8) | copy-start | bytes 6291460
  6.5 67.1 %reduce-scatter.3.cloned.1.call-start = ((), (), s32[]{:S(2)}) async-start(), calls=%async_computation.2 | async-start | bytes 196608 | tf_op jit(solution)/shard_map/reduce_scatter | solution.py:52
  6.5 68.8 %copy-start.2 = (s32[256]{0:T(256)S(1)}, s32[256]{0:T(256)}, u32[]{:S(2)}) copy-start(s32[256]{0:T(256)} %param.13) | copy-start | bytes 3076
  6.5 80.5 %copy-start.1 = (bf16[1,256,2048]{2,1,0:T(8,128)(2,1)S(1)}, bf16[1,256,2048]{2,1,0:T(8,128)(2,1)}, u32[]{:S(2)}) copy-start(bf16[1,256,2048]{2,1,0:T(8,128)(2,1)} %param.11) | copy-start | bytes 3145732
  6.5 29.5 %collective-permute-start = (bf16[256,2048]{1,0:T(8,128)(2,1)}, bf16[256,2048]{1,0:T(8,128)(2,1)}, u32[]{:S(2)}, u32[]{:S(2)}) collective-permute-start(bf16[256,2048]{1,0:T(8,128)(2,1)} %bitcast.46), channel_id=1, source_target_pairs={{0,4},{4,8},{8,12},{12,0},{1,5},{5,9},{9,13},{13,1},{2,6},{6,10},{... | collective-permute-start | bytes 3145736 | tf_op jit(solution)/shard_map/ppermute | solution.py:23
  9.7 77.4 %collective-permute-start.2 = (bf16[256,2048]{1,0:T(8,128)(2,1)}, bf16[256,2048]{1,0:T(8,128)(2,1)}, u32[]{:S(2)}, u32[]{:S(2)}) collective-permute-start(bf16[256,2048]{1,0:T(8,128)(2,1)} %bitcast.47), channel_id=1, source_target_pairs={{4,0},{8,4},{12,8},{0,12},{5,1},{9,5},{13,9},{1,13},{6,2},{10,6},{... | collective-permute-start | bytes 3145736 | tf_op jit(solution)/shard_map/ppermute | solution.py:25
  36.1 51.0 %collective-permute-start.1 = (bf16[256,2048]{1,0:T(8,128)(2,1)}, bf16[256,2048]{1,0:T(8,128)(2,1)}, u32[]{:S(2)}, u32[]{:S(2)}) collective-permute-start(bf16[256,2048]{1,0:T(8,128)(2,1)} %collective-permute-done), channel_id=1, source_target_pairs={{0,4},{4,8},{8,12},{12,0},{1,5},{5,9},{9,13},{13,1},{2,6},{6,10},{... | collective-permute-start | bytes 3145736 | tf_op jit(solution)/shard_map/ppermute | solution.py:23
  42.3 43.9 %reduce-scatter.5.cloned.1.call-start = ((), (), s32[]{:S(2)}) async-start(), calls=%async_computation.3 | async-start | bytes 49152 | tf_op jit(solution)/shard_map/reduce_scatter | solution.py:57
Sparse Core Ops, SparseCore 0:
  42.5 31.1 reduce-scatter.2
  75.8 9.9 reduce-scatter.4
